TPU v7x, 32 devices: a whole 2x2x4 slice. The times are simulated.
32 devices in a mesh: dp: 4 (over z), fsdp: 2 (over x), rows: 4 (over y, core).
Axes of the slice: x: 2, y: 2, z: 4, core: 2. Of those that a mesh axis runs over, the one named last changes fastest.
Arguments:
- feature_maps: bfloat16 [8, 16, 32, 1536], P(('dp', 'fsdp'), 'rows'), may hold values from -30 to 30
- dw_kernel: float32 [7, 7, 1536], replicated, may hold values from -0.875 to 0.875
- norm_gain: float32 [1536], replicated, may hold values from 0.5 to 1.5
- w_up: bfloat16 [1536, 6144], P(('dp', 'rows'), 'fsdp'), may hold values from -0.15625 to 0.15625
- w_down: bfloat16 [6144, 1536], P('fsdp', ('dp', 'rows')), may hold values from -0.078125 to 0.078125
- layer_scale: float32 [1536], replicated, may hold values from 0.3 to 1.5
- d_out: bfloat16 [8, 16, 32, 1536], P(('dp', 'fsdp'), 'rows'), may hold values from -20 to 20
Outputs:
- result: bfloat16 [8, 16, 32, 1536], P(('dp', 'fsdp'), 'rows')
- grad_x: bfloat16 [8, 16, 32, 1536], P(('dp', 'fsdp'), 'rows')
- grad_up: float32 [1536, 6144], P(('dp', 'rows'), 'fsdp')
- grad_down: float32 [6144, 1536], P('fsdp', ('dp', 'rows'))
- grad_kernel: float32 [7, 7, 1536], replicated
- grad_gain: float32 [1536], replicated
- grad_scale: float32 [1536], replicated
All inputs are finite; a program needn't handle non-finite values.
Results may differ from a plain program's by a relative error of at most 0.0075.
Values may be sent and summed in bfloat16 or wider, within the bound.
No kernel may reach another device: no remote copies, remote signals or barrier semaphores. Data moves between devices by JAX's collectives and lax.ppermute only.
A program may use at most 128 MiB of HBM per device.

v0:
```python
import math
import jax
import jax.numpy as jnp
from jax import lax
from jax.sharding import PartitionSpec as P

KS = 7
norm_eps = 1e-06
inv_root_two = 1.0 / math.sqrt(2.0)
inv_root_two_pi = 1.0 / math.sqrt(2.0 * math.pi)
contract_rows = (((0,), (0,)), ((), ()))
contract_cols = (((1,), (1,)), ((), ()))


def padded_2(x, sides, width):
    for axis, dim in sides:
        devices, length = (lax.axis_size(axis), x.shape[dim])
        up = [(i, (i + 1) % devices) for i in range(devices - 1)]
        down = [(j, i) for i, j in up]
        last = lax.slice_in_dim(x, length - width, length, axis=dim)
        leading = lax.slice_in_dim(x, 0, width, axis=dim)
        before = lax.ppermute(last, axis, up)
        after = lax.ppermute(leading, axis, down)
        x = jnp.concatenate([before, x, after], axis=dim)
    return x


def gelu_exact(values):
    return 0.5 * values * (1.0 + jax.scipy.special.erf(values * inv_root_two))


def gelu_slope(values):
    cdf_part = 0.5 * (1.0 + jax.scipy.special.erf(values * inv_root_two))
    return cdf_part + values * jnp.exp(-0.5 * values * values) * inv_root_two_pi


def body(feature_maps, dw_kernel, norm_gain, w_up, w_down, layer_scale, d_out):
    scenes, strip, across, width = feature_maps.shape
    cells = scenes * strip * across
    hid_axes = ("fsdp", "rows")
    up_loc = lax.all_to_all(w_up, "rows", 1, 0, tiled=True)
    up_loc = lax.all_gather(up_loc, "dp", axis=0, tiled=True)
    down_loc = lax.all_to_all(w_down, "rows", 0, 1, tiled=True)
    down_loc = lax.all_gather(down_loc, "dp", axis=1, tiled=True)
    cotan = d_out.reshape(cells, width).astype(jnp.float32)
    back = (cotan * layer_scale).astype(jnp.bfloat16)
    back_all = lax.all_gather(back, hid_axes, axis=0, tiled=True)
    rimmed = padded_2(feature_maps, (("rows", 1),), 3)
    padded = jnp.pad(rimmed.astype(jnp.float32), ((0, 0), (0, 0), (3, 3), (0, 0)))
    filtered = jnp.zeros(feature_maps.shape, jnp.float32)
    for row_off in range(KS):
        for col_off in range(KS):
            filtered = (
                filtered
                + padded[:, row_off : row_off + strip, col_off : col_off + across, :]
                * dw_kernel[row_off, col_off]
            )
    flat = filtered.reshape(cells, width)
    average = jnp.mean(flat, axis=-1, keepdims=True)
    center = flat - average
    variance = jnp.mean(center * center, axis=-1, keepdims=True)
    rstd = lax.rsqrt(variance + norm_eps)
    normed = center * rstd
    scaled = (normed * norm_gain).astype(jnp.bfloat16)
    gathered = lax.all_gather(scaled, hid_axes, axis=0, tiled=True)
    hidden = jnp.dot(gathered, up_loc, preferred_element_type=jnp.float32)
    active = gelu_exact(hidden).astype(jnp.bfloat16)
    mlp_terms = jnp.dot(active, down_loc, preferred_element_type=jnp.float32)
    branch = lax.psum_scatter(
        mlp_terms.astype(jnp.bfloat16), hid_axes, scatter_dimension=0, tiled=True
    ).astype(jnp.float32)
    resid = feature_maps.reshape(cells, width).astype(jnp.float32)
    result = (resid + layer_scale * branch).astype(jnp.bfloat16).reshape(feature_maps.shape)
    scale_part = jnp.sum(cotan * branch, axis=0)
    down_part = lax.dot_general(active, back_all, contract_rows, preferred_element_type=jnp.float32)
    slope_in = lax.dot_general(
        back_all, down_loc, contract_cols, preferred_element_type=jnp.float32
    )
    hidden_grad = (slope_in * gelu_slope(hidden)).astype(jnp.bfloat16)
    up_part = lax.dot_general(
        gathered, hidden_grad, contract_rows, preferred_element_type=jnp.float32
    )
    norm_terms = lax.dot_general(
        hidden_grad, up_loc, contract_cols, preferred_element_type=jnp.float32
    )
    norm_grad = lax.psum_scatter(norm_terms, hid_axes, scatter_dimension=0, tiled=True)
    grad_up = lax.psum_scatter(up_part, "dp", scatter_dimension=0, tiled=True)
    grad_up = lax.all_to_all(grad_up, "rows", 0, 1, tiled=True)
    grad_down = lax.psum_scatter(down_part, "dp", scatter_dimension=1, tiled=True)
    grad_down = lax.all_to_all(grad_down, "rows", 1, 0, tiled=True)
    gain_part = jnp.sum(norm_grad * normed, axis=0)
    scaled_grad = norm_grad * norm_gain
    conv_grad = rstd * (
        scaled_grad
        - jnp.mean(scaled_grad, axis=-1, keepdims=True)
        - normed * jnp.mean(scaled_grad * normed, axis=-1, keepdims=True)
    )
    conv_grad = conv_grad.reshape(feature_maps.shape)
    grad_rim = padded_2(conv_grad.astype(jnp.bfloat16), (("rows", 1),), 3).astype(conv_grad.dtype)
    grad_pad = jnp.pad(grad_rim, ((0, 0), (0, 0), (3, 3), (0, 0)))
    kernel_rows = []
    back_conv = jnp.zeros(feature_maps.shape, jnp.float32)
    for row_off in range(KS):
        for col_off in range(KS):
            window = padded[:, row_off : row_off + strip, col_off : col_off + across, :]
            kernel_rows.append(jnp.sum(window * conv_grad, axis=(0, 1, 2)))
            back_conv = (
                back_conv
                + grad_pad[
                    :, 6 - row_off : 6 - row_off + strip, 6 - col_off : 6 - col_off + across, :
                ]
                * dw_kernel[row_off, col_off]
            )
    kernel_part = jnp.stack(kernel_rows).reshape(KS, KS, width)
    grad_x = (d_out.astype(jnp.float32) + back_conv).astype(jnp.bfloat16)
    grad_kernel, grad_gain, grad_scale = lax.psum(
        (kernel_part, gain_part, scale_part), ("dp", "fsdp", "rows")
    )
    return (result, grad_x, grad_up, grad_down, grad_kernel, grad_gain, grad_scale)


def solution(mesh):
    return jax.shard_map(
        body,
        mesh=mesh,
        in_specs=(
            P(("dp", "fsdp"), "rows", None, None),
            P(),
            P(),
            P(("dp", "rows"), "fsdp"),
            P("fsdp", ("dp", "rows")),
            P(),
            P(("dp", "fsdp"), "rows", None, None),
        ),
        out_specs=(
            P(("dp", "fsdp"), "rows", None, None),
            P(("dp", "fsdp"), "rows", None, None),
            P(("dp", "rows"), "fsdp"),
            P("fsdp", ("dp", "rows")),
            P(),
            P(),
            P(),
        ),
        check_vma=False,
    )
```

profile of v0, /device:TPU:1, one launch (start us, length us, event | category | flops | bytes accessed | tf_op | source)
XLA Modules:
  0.0 634.2 jit_solution(6933835637550639418)
XLA Ops:
  7.2 1.2 copy.35
  8.4 13.0 %all_to_all.76 = bf16[96,4,768]{2,0,1:T(8,128)(2,1)} all-to-all(bf16[96,4,768]{2,0,1:T(8,128)(2,1)S(1)} %bitcast.112), channel_id=1, replica_groups=mesh['dp'=4,'fsdp'=2,'rows'=4] {'rows'}, dimensions={1} | all-to-all | bytes 1179648 | tf_op jit(solution)/shard_map/all_to_all | solution.py:41
  21.5 2.6 collective-permute-start
  24.2 1.9 collective-permute-start.1
  26.9 0.9 slice_reduce_fusion.47
  27.9 4.3 collective-permute-done.1
  32.4 9.5 %fusion.103 = (f32[4,32]{1,0:T(4,128)S(1)}, f32[1,4,32,1536]{3,2,1,0:T(8,128)S(1)}) fusion(f32[1536]{0:T(1024)S(1)} %get-tuple-element.106, f32[1536]{0:T(1024)S(1)} %get-tuple-element.107, f32[1536]{0:T(1024)S(1)} %get-tuple-element.60, f32[1536]{0:T(1024)S(1)} %get-tuple-element.61, f32[1,10,32,1536]{3,2,1,0:T(8,128)S(1)} %maximum_convert_fusion, ...), kind=kLoop, calls=%fused_computation.315 | loop fusion | flops 19267456 | bytes 8641024 | tf_op jit(solution)/shard_map/reduce_sum | solution.py:59
  42.6 0.9 multiply_convert_fusion.1
  43.6 1.1 copy.34
  44.7 10.7 %all_to_all.77 = bf16[4,768,96]{1,2,0:T(8,128)(2,1)} all-to-all(bf16[4,768,96]{1,2,0:T(8,128)(2,1)S(1)} %bitcast.113), channel_id=1, replica_groups=mesh['dp'=4,'fsdp'=2,'rows'=4] {'rows'}, dimensions={0} | all-to-all | bytes 1179648 | tf_op jit(solution)/shard_map/all_to_all | solution.py:43
  55.5 17.3 %all-gather.7.cloned.1.call-done = bf16[1536,768]{1,0:T(8,128)(2,1)} async-done(((bf16[384,768]{1,0:T(8,128)(2,1)}), bf16[1536,768]{1,0:T(8,128)(2,1)}) %all-gather.7.cloned.1.call-update) | async-done | bytes 2359312 | tf_op jit(solution)/shard_map/all_gather | solution.py:42
  72.8 34.1 %all-gather.5.cloned.1.call-done = bf16[1024,1536]{1,0:T(8,128)(2,1)} async-done(((bf16[128,1536]{1,0:T(8,128)(2,1)}), bf16[1024,1536]{1,0:T(8,128)(2,1)}) %all-gather.5.cloned.1.call-update) | async-done | bytes 3145744 | tf_op jit(solution)/shard_map/all_gather | solution.py:65
  106.9 7.4 %multiply_convert_fusion = (bf16[1024,768]{1,0:T(8,128)(2,1)}, f32[1024,768]{1,0:T(8,128)}) fusion(bf16[1024,1536]{1,0:T(8,128)(2,1)} %all-gather.5.cloned.1.call-done, bf16[1536,768]{1,0:T(8,128)(2,1)} %all-gather.7.cloned.1.call-done), kind=kOutput, calls=%fused_computation.92 | convolution fusion | flops 2419851264 | bytes 10223616 | tf_op jit(solution)/shard_map/dot_general | solution.py:66
  114.3 44.2 %all-gather.9.cloned.1.call-done = bf16[768,1536]{0,1:T(8,128)(2,1)} async-done(((bf16[768,384]{0,1:T(8,128)(2,1)}), bf16[768,1536]{0,1:T(8,128)(2,1)}) %all-gather.9.cloned.1.call-update) | async-done | bytes 2359312 | tf_op jit(solution)/shard_map/all_gather | solution.py:44
  158.5 6.5 %convolution_convert_fusion = bf16[1024,1536]{1,0:T(8,128)(2,1)} fusion(bf16[1024,768]{1,0:T(8,128)(2,1)} %get-tuple-element.120, bf16[768,1536]{0,1:T(8,128)(2,1)} %all-gather.9.cloned.1.call-done), kind=kOutput, calls=%fused_computation.85 | convolution fusion | flops 2417491968 | bytes 7077888 | tf_op jit(solution)/shard_map/dot_general | solution.py:68
  165.1 45.2 %reduce-scatter.5.cloned.1.call-done = bf16[128,1536]{1,0:T(8,128)(2,1)} async-done(((bf16[1024,1536]{1,0:T(8,128)(2,1)}), bf16[128,1536]{1,0:T(8,128)(2,1)}) %reduce-scatter.5.cloned.1.call-update) | async-done | bytes 393232 | tf_op jit(solution)/shard_map/reduce_scatter | solution.py:69
  210.2 2.7 fusion.8
  213.2 32.7 %all-gather.11.cloned.1.call-done = bf16[1024,1536]{1,0:T(8,128)(2,1)} async-done(((bf16[128,1536]{1,0:T(8,128)(2,1)}), bf16[1024,1536]{1,0:T(8,128)(2,1)}) %all-gather.11.cloned.1.call-update) | async-done | bytes 3145744 | tf_op jit(solution)/shard_map/all_gather | solution.py:47
  245.9 7.2 %fusion.108 = f32[768,1536]{1,0:T(8,128)} fusion(bf16[1024,768]{1,0:T(8,128)(2,1)} %get-tuple-element.120, bf16[1024,1536]{1,0:T(8,128)(2,1)} %all-gather.11.cloned.1.call-done), kind=kOutput, calls=%fused_computation.320 | convolution fusion | flops 2415919104 | bytes 9437184 | tf_op jit(solution)/shard_map/dot_general | solution.py:75
  253.1 6.8 %fusion.5 = bf16[1024,768]{1,0:T(8,128)(2,1)S(1)} fusion(f32[1024,768]{1,0:T(8,128)} %get-tuple-element.121, bf16[1024,1536]{1,0:T(8,128)(2,1)} %all-gather.11.cloned.1.call-done, bf16[768,1536]{0,1:T(8,128)(2,1)} %all-gather.9.cloned.1.call-done), kind=kOutput, calls=%fused_computation.91 | convolution fusion | flops 2423783424 | bytes 10223616 | tf_op jit(solution)/shard_map/dot_general | solution.py:76
  260.0 1.2 copy-done.49
  261.1 4.6 fusion.106
  265.8 7.2 %fusion.107 = f32[1536,768]{1,0:T(8,128)} fusion(bf16[1024,1536]{1,0:T(8,128)(2,1)} %all-gather.5.cloned.1.call-done, bf16[1024,768]{1,0:T(8,128)(2,1)} %copy-done.49), kind=kOutput, calls=%fused_computation.319 | convolution fusion | flops 2415919104 | bytes 9437184 | tf_op jit(solution)/shard_map/dot_general | solution.py:80
  273.0 65.1 %reduce-scatter.11.cloned.1.call-done = f32[768,384]{1,0:T(8,128)} async-done(((f32[768,1536]{1,0:T(8,128)}), f32[768,384]{1,0:T(8,128)}) %reduce-scatter.11.cloned.1.call-update) | async-done | bytes 1179664 | tf_op jit(solution)/shard_map/reduce_scatter | solution.py:89
  338.1 2.7 copy.26
  340.8 4.9 all-to-all-start.3
  345.7 58.4 %reduce-scatter.7.cloned.1.call-done = f32[128,1536]{1,0:T(8,128)} async-done(((f32[1024,1536]{1,0:T(8,128)}), f32[128,1536]{1,0:T(8,128)}) %reduce-scatter.7.cloned.1.call-update) | async-done | bytes 786448 | tf_op jit(solution)/shard_map/reduce_scatter | solution.py:86
  404.1 2.0 multiply_reduce_fusion
  406.2 3.6 multiply_reduce_fusion.2
  409.8 2.0 multiply_reduce_fusion.1
  411.8 0.9 fusion.104
  414.5 0.6 stack.172
  416.3 0.6 stack.176
  420.5 0.6 stack.184
  424.1 3.6 collective-permute-start.2
  427.7 1.9 collective-permute-start.3
  429.6 1.1 multiply_reduce_fusion.3
  431.2 4.2 stack.199
  435.4 0.8 reshape.335
  436.2 46.1 %all-reduce.2 = (f32[1536]{0:T(1024)}, f32[1536]{0:T(1024)}) all-reduce(f32[1536]{0:T(1024)} %get-tuple-element.56, f32[1536]{0:T(1024)} %get-tuple-element.113), channel_id=1, replica_groups=mesh['dp'=4,'fsdp'=2,'rows'=4] {'dp','fsdp','rows'}, use_global_device_ids=true, to_apply=%region_59.60 | all-reduce | flops 3072 | bytes 24576 | tf_op jit(solution)/shard_map/psum | solution.py:116
  482.4 10.4 %reduce-scatter.9.cloned.1.call-done = f32[384,768]{1,0:T(8,128)} async-done(((f32[1536,768]{1,0:T(8,128)}), f32[384,768]{1,0:T(8,128)}) %reduce-scatter.9.cloned.1.call-update) | async-done | bytes 1179664 | tf_op jit(solution)/shard_map/reduce_scatter | solution.py:87
  492.8 4.1 all-to-all-start.2
  496.9 8.0 %fusion.96 = bf16[1,4,32,1536]{3,2,1,0:T(8,128)(2,1)} fusion(f32[1,10,32,1536]{3,2,1,0:T(8,128)S(1)} %maximum_convert_fusion.1, bf16[1,4,32,1536]{3,2,1,0:T(8,128)(2,1)S(1)} %copy-done.1, f32[1536]{0:T(1024)} %copy-done.13, f32[1536]{0:T(1024)} %copy-done.14, f32[1536]{0:T(1024)} %copy-done.16, f32[1536]{0:T(1024)} %copy-done.17, f32[1536]{0:T(1024)} %copy-done.18, ...), kind=kLoop, calls=%fused_computation.188 | loop fusion | flops 19660800 | bytes 8562688 | tf_op jit(solution)/shard_map/convert_element_type | solution.py:115
  504.9 2.4 copy.31
  507.3 5.2 all-to-all-done.2
  512.5 1.1 copy.30
  513.7 112.3 %all-reduce.5.cloned.1.call-done = f32[7,7,1536]{2,1,0:T(8,128)} async-done(((f32[7,7,1536]{2,1,0:T(8,128)}), f32[7,7,1536]{2,1,0:T(8,128)}) %all-reduce.5.cloned.1.call-update) | async-done | bytes 301072 | tf_op jit(solution)/shard_map/psum | solution.py:116
  626.0 1.7 copy.37
  (180 shorter events, 11.9 us)
Async XLA Ops:
  7.2 18.9 %copy-start.2 = (f32[7,7,1536]{2,1,0:T(8,128)S(1)}, f32[7,7,1536]{2,1,0:T(8,128)}, u32[]{:S(2)}) copy-start(f32[7,7,1536]{2,1,0:T(8,128)} %param.8) | copy-start | bytes 903172
  7.2 65.6 %all-gather.7.cloned.1.call-start = ((), (), s32[]{:S(2)}) async-start(), calls=%async_computation.9 | async-start | bytes 2949120 | tf_op jit(solution)/shard_map/all_gather | solution.py:42
  21.4 85.5 %all-gather.5.cloned.1.call-start = ((), (), s32[]{:S(2)}) async-start(), calls=%async_computation.8 | async-start | bytes 3538944 | tf_op jit(solution)/shard_map/all_gather | solution.py:65
  21.5 6.3 %collective-permute-start = (bf16[1,3,32,1536]{3,2,1,0:T(8,128)(2,1)S(1)}, bf16[1,3,32,1536]{3,2,1,0:T(8,128)(2,1)S(1)}, u32[]{:S(2)}, u32[]{:S(2)}) collective-permute-start(bf16[1,3,32,1536]{3,2,1,0:T(8,128)(2,1)S(1)} %get-tuple-element.118), channel_id=1, source_target_pairs={{0,1},{1,2},{2,3},{4,5},{5,6},{6,7},{8,9},{9,10},{10,11},{12,13},{... | collective-permute-start | bytes 884744 | tf_op jit(solution)/shard_map/ppermute | solution.py:22
  24.2 8.0 %collective-permute-start.1 = (bf16[1,3,32,1536]{3,2,1,0:T(8,128)(2,1)S(1)}, bf16[1,3,32,1536]{3,2,1,0:T(8,128)(2,1)S(1)}, u32[]{:S(2)}, u32[]{:S(2)}) collective-permute-start(bf16[1,3,32,1536]{3,2,1,0:T(8,128)(2,1)S(1)} %get-tuple-element.119), channel_id=1, source_target_pairs={{1,0},{2,1},{3,2},{5,4},{6,5},{7,6},{9,8},{10,9},{11,10},{13,12},{... | collective-permute-start | bytes 884744 | tf_op jit(solution)/shard_map/ppermute | solution.py:23
  26.3 15.5 %copy-start.4 = (f32[1536]{0:T(1024)}, f32[1536]{0:T(1024)S(1)}, u32[]{:S(2)}) copy-start(f32[1536]{0:T(1024)S(1)} %get-tuple-element.98) | copy-start | bytes 18436
  26.3 15.5 %copy-start.6 = (f32[1536]{0:T(1024)}, f32[1536]{0:T(1024)S(1)}, u32[]{:S(2)}) copy-start(f32[1536]{0:T(1024)S(1)} %get-tuple-element.99) | copy-start | bytes 18436
  26.3 15.5 %copy-start.7 = (f32[1536]{0:T(1024)}, f32[1536]{0:T(1024)S(1)}, u32[]{:S(2)}) copy-start(f32[1536]{0:T(1024)S(1)} %get-tuple-element.100) | copy-start | bytes 18436
  26.3 15.5 %copy-start.8 = (f32[1536]{0:T(1024)}, f32[1536]{0:T(1024)S(1)}, u32[]{:S(2)}) copy-start(f32[1536]{0:T(1024)S(1)} %get-tuple-element.101) | copy-start | bytes 18436
  26.3 15.5 %copy-start.9 = (f32[1536]{0:T(1024)}, f32[1536]{0:T(1024)S(1)}, u32[]{:S(2)}) copy-start(f32[1536]{0:T(1024)S(1)} %get-tuple-element.102) | copy-start | bytes 18436
  26.3 15.5 %copy-start.10 = (f32[1536]{0:T(1024)}, f32[1536]{0:T(1024)S(1)}, u32[]{:S(2)}) copy-start(f32[1536]{0:T(1024)S(1)} %get-tuple-element.103) | copy-start | bytes 18436
  26.4 15.5 %copy-start.11 = (f32[1536]{0:T(1024)}, f32[1536]{0:T(1024)S(1)}, u32[]{:S(2)}) copy-start(f32[1536]{0:T(1024)S(1)} %get-tuple-element.104) | copy-start | bytes 18436
  26.4 15.5 %copy-start.12 = (f32[1536]{0:T(1024)}, f32[1536]{0:T(1024)S(1)}, u32[]{:S(2)}) copy-start(f32[1536]{0:T(1024)S(1)} %get-tuple-element.105) | copy-start | bytes 18436
  26.4 15.5 %copy-start.13 = (f32[1536]{0:T(1024)}, f32[1536]{0:T(1024)S(1)}, u32[]{:S(2)}) copy-start(f32[1536]{0:T(1024)S(1)} %get-tuple-element.106) | copy-start | bytes 18436
  26.4 15.5 %copy-start.14 = (f32[1536]{0:T(1024)}, f32[1536]{0:T(1024)S(1)}, u32[]{:S(2)}) copy-start(f32[1536]{0:T(1024)S(1)} %get-tuple-element.107) | copy-start | bytes 18436
  26.7 15.2 %copy-start.15 = (f32[1536]{0:T(1024)}, f32[1536]{0:T(1024)S(1)}, u32[]{:S(2)}) copy-start(f32[1536]{0:T(1024)S(1)} %get-tuple-element.59) | copy-start | bytes 18436
  26.7 15.2 %copy-start.16 = (f32[1536]{0:T(1024)}, f32[1536]{0:T(1024)S(1)}, u32[]{:S(2)}) copy-start(f32[1536]{0:T(1024)S(1)} %get-tuple-element.60) | copy-start | bytes 18436
  26.7 15.2 %copy-start.17 = (f32[1536]{0:T(1024)}, f32[1536]{0:T(1024)S(1)}, u32[]{:S(2)}) copy-start(f32[1536]{0:T(1024)S(1)} %get-tuple-element.61) | copy-start | bytes 18436
  26.7 15.2 %copy-start.18 = (f32[1536]{0:T(1024)}, f32[1536]{0:T(1024)S(1)}, u32[]{:S(2)}) copy-start(f32[1536]{0:T(1024)S(1)} %get-tuple-element.62) | copy-start | bytes 18436
  26.8 15.2 %copy-start.19 = (f32[1536]{0:T(1024)}, f32[1536]{0:T(1024)S(1)}, u32[]{:S(2)}) copy-start(f32[1536]{0:T(1024)S(1)} %get-tuple-element.63) | copy-start | bytes 18436
  26.8 15.2 %copy-start.20 = (f32[1536]{0:T(1024)}, f32[1536]{0:T(1024)S(1)}, u32[]{:S(2)}) copy-start(f32[1536]{0:T(1024)S(1)} %get-tuple-element.64) | copy-start | bytes 18436
  26.8 15.2 %copy-start.21 = (f32[1536]{0:T(1024)}, f32[1536]{0:T(1024)S(1)}, u32[]{:S(2)}) copy-start(f32[1536]{0:T(1024)S(1)} %get-tuple-element.65) | copy-start | bytes 18436
  26.8 15.2 %copy-start.22 = (f32[1536]{0:T(1024)}, f32[1536]{0:T(1024)S(1)}, u32[]{:S(2)}) copy-start(f32[1536]{0:T(1024)S(1)} %get-tuple-element.66) | copy-start | bytes 18436
  26.8 15.2 %copy-start.23 = (f32[1536]{0:T(1024)}, f32[1536]{0:T(1024)S(1)}, u32[]{:S(2)}) copy-start(f32[1536]{0:T(1024)S(1)} %get-tuple-element.67) | copy-start | bytes 18436
  26.8 15.2 %copy-start.24 = (f32[1536]{0:T(1024)}, f32[1536]{0:T(1024)S(1)}, u32[]{:S(2)}) copy-start(f32[1536]{0:T(1024)S(1)} %get-tuple-element.68) | copy-start | bytes 18436
  26.8 15.2 %copy-start.25 = (f32[1536]{0:T(1024)}, f32[1536]{0:T(1024)S(1)}, u32[]{:S(2)}) copy-start(f32[1536]{0:T(1024)S(1)} %get-tuple-element.69) | copy-start | bytes 18436
  26.8 15.2 %copy-start.26 = (f32[1536]{0:T(1024)}, f32[1536]{0:T(1024)S(1)}, u32[]{:S(2)}) copy-start(f32[1536]{0:T(1024)S(1)} %get-tuple-element.70) | copy-start | bytes 18436
  26.8 15.2 %copy-start.27 = (f32[1536]{0:T(1024)}, f32[1536]{0:T(1024)S(1)}, u32[]{:S(2)}) copy-start(f32[1536]{0:T(1024)S(1)} %get-tuple-element.71) | copy-start | bytes 18436
  26.8 15.2 %copy-start.28 = (f32[1536]{0:T(1024)}, f32[1536]{0:T(1024)S(1)}, u32[]{:S(2)}) copy-start(f32[1536]{0:T(1024)S(1)} %get-tuple-element.72) | copy-start | bytes 18436
  26.9 15.2 %copy-start.29 = (f32[1536]{0:T(1024)}, f32[1536]{0:T(1024)S(1)}, u32[]{:S(2)}) copy-start(f32[1536]{0:T(1024)S(1)} %get-tuple-element.73) | copy-start | bytes 18436
  26.9 15.2 %copy-start.30 = (f32[1536]{0:T(1024)}, f32[1536]{0:T(1024)S(1)}, u32[]{:S(2)}) copy-start(f32[1536]{0:T(1024)S(1)} %get-tuple-element.74) | copy-start | bytes 18436
  26.9 15.2 %copy-start.31 = (f32[1536]{0:T(1024)}, f32[1536]{0:T(1024)S(1)}, u32[]{:S(2)}) copy-start(f32[1536]{0:T(1024)S(1)} %get-tuple-element.75) | copy-start | bytes 18436
  26.9 15.2 %copy-start.32 = (f32[1536]{0:T(1024)}, f32[1536]{0:T(1024)S(1)}, u32[]{:S(2)}) copy-start(f32[1536]{0:T(1024)S(1)} %get-tuple-element.76) | copy-start | bytes 18436
  42.6 71.7 %copy-start.46 = (f32[128]{0:T(128)}, f32[128]{0:T(128)S(1)}, u32[]{:S(2)}) copy-start(f32[128]{0:T(128)S(1)} %rsqrt.12) | copy-start | bytes 1540
  43.6 114.9 %all-gather.9.cloned.1.call-start = ((), (), s32[]{:S(2)}) async-start(), calls=%async_computation.10 | async-start | bytes 2949120 | tf_op jit(solution)/shard_map/all_gather | solution.py:44
  55.4 154.8 %reduce-scatter.5.cloned.1.call-start = ((), (), s32[]{:S(2)}) async-start(), calls=%async_computation.11 | async-start | bytes 3538944 | tf_op jit(solution)/shard_map/reduce_scatter | solution.py:69
  165.0 45.2 %copy-start.1 = (bf16[1,4,32,1536]{3,2,1,0:T(8,128)(2,1)S(1)}, bf16[1,4,32,1536]{3,2,1,0:T(8,128)(2,1)}, u32[]{:S(2)}) copy-start(bf16[1,4,32,1536]{3,2,1,0:T(8,128)(2,1)} %param.13) | copy-start | bytes 1179652
  165.0 80.8 %all-gather.11.cloned.1.call-start = ((), (), s32[]{:S(2)}) async-start(), calls=%async_computation.12 | async-start | bytes 3538944 | tf_op jit(solution)/shard_map/all_gather | solution.py:47
  213.0 125.2 %reduce-scatter.11.cloned.1.call-start = ((), (), s32[]{:S(2)}) async-start(), calls=%async_computation.15 | async-start | bytes 5898240 | tf_op jit(solution)/shard_map/reduce_scatter | solution.py:89
  253.1 151.0 %reduce-scatter.7.cloned.1.call-start = ((), (), s32[]{:S(2)}) async-start(), calls=%async_computation.13 | async-start | bytes 7077888 | tf_op jit(solution)/shard_map/reduce_scatter | solution.py:86
  265.7 227.1 %reduce-scatter.9.cloned.1.call-start = ((), (), s32[]{:S(2)}) async-start(), calls=%async_computation.14 | async-start | bytes 5898240 | tf_op jit(solution)/shard_map/reduce_scatter | solution.py:87
  273.0 131.1 %copy-start.45 = (f32[128]{0:T(128)S(1)}, f32[128]{0:T(128)}, u32[]{:S(2)}) copy-start(f32[128]{0:T(128)} %copy-done.44) | copy-start | bytes 1540
  273.0 131.1 %copy-start.47 = (f32[128]{0:T(128)S(1)}, f32[128]{0:T(128)}, u32[]{:S(2)}) copy-start(f32[128]{0:T(128)} %copy-done.46) | copy-start | bytes 1540
  340.8 152.0 %all-to-all-start.3 = ((f32[768,4,96]{0,2,1:T(8,128)}), f32[768,4,96]{0,2,1:T(8,128)}, u32[]{:S(2)}, u32[]{:S(2)}) async-start(f32[768,4,96]{0,2,1:T(8,128)} %bitcast.108), calls=%async_computation.7 | async-start | bytes 2359296 | tf_op jit(solution)/shard_map/all_to_all | solution.py:90
  345.7 280.3 %all-reduce.5.cloned.1.call-start = ((), (), s32[]{:S(2)}) async-start(), calls=%async_computation.16 | async-start | bytes 688128 | tf_op jit(solution)/shard_map/psum | solution.py:116
  424.1 58.2 %collective-permute-start.2 = (bf16[1,3,32,1536]{3,2,1,0:T(8,128)(2,1)}, bf16[1,3,32,1536]{3,2,1,0:T(8,128)(2,1)S(1)}, u32[]{:S(2)}, u32[]{:S(2)}) collective-permute-start(bf16[1,3,32,1536]{3,2,1,0:T(8,128)(2,1)} %get-tuple-element.116), channel_id=1, source_target_pairs={{0,1},{1,2},{2,3},{4,5},{5,6},{6,7},{8,9},{9,10},{10,11},{12,13},{... | collective-permute-start | bytes 884744 | tf_op jit(solution)/shard_map/ppermute | solution.py:22
  427.7 54.6 %collective-permute-start.3 = (bf16[1,3,32,1536]{3,2,1,0:T(8,128)(2,1)}, bf16[1,3,32,1536]{3,2,1,0:T(8,128)(2,1)S(1)}, u32[]{:S(2)}, u32[]{:S(2)}) collective-permute-start(bf16[1,3,32,1536]{3,2,1,0:T(8,128)(2,1)} %get-tuple-element.117), channel_id=1, source_target_pairs={{1,0},{2,1},{3,2},{5,4},{6,5},{7,6},{9,8},{10,9},{11,10},{13,12},{... | collective-permute-start | bytes 884744 | tf_op jit(solution)/shard_map/ppermute | solution.py:23
  492.8 19.8 %all-to-all-start.2 = ((f32[4,96,768]{2,1,0:T(8,128)}), f32[4,96,768]{2,1,0:T(8,128)S(1)}, u32[]{:S(2)}, u32[]{:S(2)}) async-start(f32[4,96,768]{2,1,0:T(8,128)} %bitcast.115), calls=%async_computation.5 | async-start | bytes 2359296 | tf_op jit(solution)/shard_map/all_to_all | solution.py:88
  (17 other events, 220.0 us)
Sparse Core Ops, SparseCore 0:
  21.5 51.2 all-gather.6
  75.3 31.5 all-gather.4
  108.5 50.0 all-gather.8
  165.1 45.0 reduce-scatter.4
  213.1 32.7 all-gather.10
  253.2 84.8 reduce-scatter.10
  341.9 62.1 reduce-scatter.6
  406.4 86.3 reduce-scatter.8
  498.7 127.2 all-reduce.4
where the time goes:
time: 635 us; the launch traced here: 634 us
  waiting for transfers between devices  429 us (68%)
  blocking collectives  69.8 us (11%)
  matrix products  39.7 us (6%)
  local copies, waits for them, and re-layouts  30.5 us (5%)
  other arithmetic  30.4 us (5%)
  starting transfers between devices  19.6 us (3%)
  between operations  14.9 us (2%)
    psum x1, waiting for transfers between devices, body(): lax.psum((kernel_part, gain_part, scale_part), ('dp', 'fsdp', 'rows'))  112 us
    reduce_scatter x1, waiting for transfers between devices, body(): lax.psum_scatter(down_part, 'dp', scatter_dimension=1, tiled=True)  65.1 us
    reduce_scatter x1, waiting for transfers between devices, body(): lax.psum_scatter(norm_terms, hid_axes, scatter_dimension=0, tiled=True)  58.4 us
    psum x1, blocking collectives, body(): lax.psum((kernel_part, gain_part, scale_part), ('dp', 'fsdp', 'rows'))  46.1 us
    reduce_scatter x1, waiting for transfers between devices, body(): lax.psum_scatter(mlp_terms.astype(jnp.bfloat16), hid_axes, scatter_dimens...  45.2 us
    all_gather x1, waiting for transfers between devices, body(): down_loc = lax.all_gather(down_loc, 'dp', axis=1, tiled=True)  44.2 us
    all_gather x1, waiting for transfers between devices, body(): gathered = lax.all_gather(scaled, hid_axes, axis=0, tiled=True)  34.1 us
    all_gather x1, waiting for transfers between devices, body(): back_all = lax.all_gather(back, hid_axes, axis=0, tiled=True)  32.7 us
  transfers between devices with their start and end apart: 15, of which 11 were waited for; matrix products, arithmetic and copies ran while one was open for 13% of the time, Pallas kernels for 0%

commit v1 on v0

--- a/solution.py
+++ b/solution.py
@@ -41,7 +41,16 @@
     up_loc = lax.all_to_all(w_up, "rows", 1, 0, tiled=True)
     up_loc = lax.all_gather(up_loc, "dp", axis=0, tiled=True)
     down_loc = lax.all_to_all(w_down, "rows", 0, 1, tiled=True)
-    down_loc = lax.all_gather(down_loc, "dp", axis=1, tiled=True)
+    size_here = lax.axis_size("dp")
+    low = [(ix - 1, ix) for ix in range(1, size_here)] + [(size_here - 1, 0)]
+    piece_out = down_loc
+    ledger = [piece_out]
+    for _ in range(size_here - 1):
+        piece_out = lax.ppermute(piece_out, "dp", low)
+        ledger += [piece_out]
+    down_loc = jnp.roll(
+        jnp.concatenate([*reversed(ledger)], 1), (lax.axis_index("dp") + 1) * piece_out.shape[1], 1
+    )
     cotan = d_out.reshape(cells, width).astype(jnp.float32)
     back = (cotan * layer_scale).astype(jnp.bfloat16)
     back_all = lax.all_gather(back, hid_axes, axis=0, tiled=True)

time: 635 us -> 613 us (0.965)
  waiting for transfers between devices: 429 us -> 393 us
  local copies, waits for them, and re-layouts: 30.5 us -> 41.4 us
    ppermute x0 -> x3, waiting for transfers between devices: none -> 59.4 us  [body(): piece_out = lax.ppermute(piece_out, 'dp', low)]
    all_gather x1 -> x0, waiting for transfers between devices: 44.2 us -> none  [body(): down_loc = lax.all_gather(down_loc, 'dp', axis=1, tiled=True)]
    all_gather x1, waiting for transfers between devices: 34.1 us -> 0.01 us  [body(): gathered = lax.all_gather(scaled, hid_axes, axis=0, tiled=True)]
    all_gather x1, waiting for transfers between devices: 17.3 us -> 0.01 us  [body(): up_loc = lax.all_gather(up_loc, 'dp', axis=0, tiled=True)]
    unnamed x101 -> x116, local copies, waits for them, and re-layouts: 3.09 us -> 14.2 us
  transfers between devices with their start and end apart: 15 -> 17, of which waited for: 11 -> 11; matrix products, arithmetic and copies ran while one was open for 13% -> 14% of each run, Pallas kernels for 0% -> 0%
where the time goes in v1:
time: 613 us; the launch traced here: 612 us
  waiting for transfers between devices  393 us (64%)
  blocking collectives  69.8 us (11%)
  local copies, waits for them, and re-layouts  41.4 us (7%)
  matrix products  39.9 us (7%)
  other arithmetic  31.4 us (5%)
  starting transfers between devices  21.2 us (3%)
  between operations  15.2 us (2%)
    psum x1, waiting for transfers between devices, body(): lax.psum((kernel_part, gain_part, scale_part), ('dp', 'fsdp', 'rows'))  112 us
    reduce_scatter x1, waiting for transfers between devices, body(): lax.psum_scatter(down_part, 'dp', scatter_dimension=1, tiled=True)  64.9 us
    ppermute x3, waiting for transfers between devices, body(): piece_out = lax.ppermute(piece_out, 'dp', low)  59.4 us
    reduce_scatter x1, waiting for transfers between devices, body(): lax.psum_scatter(norm_terms, hid_axes, scatter_dimension=0, tiled=True)  58.3 us
    reduce_scatter x1, waiting for transfers between devices, body(): lax.psum_scatter(mlp_terms.astype(jnp.bfloat16), hid_axes, scatter_dimens...  46.5 us
    psum x1, blocking collectives, body(): lax.psum((kernel_part, gain_part, scale_part), ('dp', 'fsdp', 'rows'))  46.1 us
    all_gather x1, waiting for transfers between devices, body(): back_all = lax.all_gather(back, hid_axes, axis=0, tiled=True)  32.6 us
    another operation x50, local copies, waits for them, and re-layouts, body(): kernel_part = jnp.stack(kernel_rows).reshape(KS, KS, width)  15.7 us
  transfers between devices with their start and end apart: 17, of which 11 were waited for; matrix products, arithmetic and copies ran while one was open for 14% of the time, Pallas kernels for 0%

profile of v1, /device:TPU:1, one launch (start us, length us, event | category | flops | bytes accessed | tf_op | source)
XLA Modules:
  0.0 612.0 jit_solution(3413248072680261961)
XLA Ops:
  7.2 1.2 copy.35
  8.4 13.0 %all_to_all.76 = bf16[96,4,768]{2,0,1:T(8,128)(2,1)} all-to-all(bf16[96,4,768]{2,0,1:T(8,128)(2,1)S(1)} %bitcast.112), channel_id=1, replica_groups=mesh['dp'=4,'fsdp'=2,'rows'=4] {'rows'}, dimensions={1} | all-to-all | bytes 1179648 | tf_op jit(solution)/shard_map/all_to_all | solution.py:41
  21.5 2.6 collective-permute-start
  24.2 1.9 collective-permute-start.1
  26.9 0.9 slice_reduce_fusion.47
  27.9 4.3 collective-permute-done.1
  32.8 9.4 %fusion.110 = (f32[4,32]{1,0:T(4,128)S(1)}, f32[1,4,32,1536]{3,2,1,0:T(8,128)S(1)}) fusion(f32[1536]{0:T(1024)S(1)} %get-tuple-element.106, f32[1536]{0:T(1024)S(1)} %get-tuple-element.107, f32[1536]{0:T(1024)S(1)} %get-tuple-element.60, f32[1536]{0:T(1024)S(1)} %get-tuple-element.61, f32[1,10,32,1536]{3,2,1,0:T(8,128)S(1)} %maximum_convert_fusion, ...), kind=kLoop, calls=%fused_computation.328 | loop fusion | flops 19267456 | bytes 8641024 | tf_op jit(solution)/shard_map/reduce_sum | solution.py:68
  42.6 0.9 multiply_convert_fusion.1
  43.7 10.7 %all_to_all.77 = bf16[4,768,96]{1,2,0:T(8,128)(2,1)S(1)} all-to-all(bf16[4,768,96]{1,2,0:T(8,128)(2,1)S(1)} %bitcast.113), channel_id=1, replica_groups=mesh['dp'=4,'fsdp'=2,'rows'=4] {'rows'}, dimensions={0} | all-to-all | bytes 1179648 | tf_op jit(solution)/shard_map/all_to_all | solution.py:43
  54.4 1.7 collective-permute-start.2
  56.1 28.7 %collective-permute-done.2 = bf16[768,384]{0,1:T(8,128)(2,1)S(1)} collective-permute-done((bf16[768,384]{0,1:T(8,128)(2,1)S(1)}, bf16[768,384]{0,1:T(8,128)(2,1)S(1)}, u32[]{:S(2)}, u32[]{:S(2)}) %collective-permute-start.2) | collective-permute-done | bytes 589856 | tf_op jit(solution)/shard_map/ppermute | solution.py:49
  85.6 15.7 %collective-permute-done.3 = bf16[768,384]{0,1:T(8,128)(2,1)} collective-permute-done((bf16[768,384]{0,1:T(8,128)(2,1)S(1)}, bf16[768,384]{0,1:T(8,128)(2,1)}, u32[]{:S(2)}, u32[]{:S(2)}) %collective-permute-start.3) | collective-permute-done | bytes 589856 | tf_op jit(solution)/shard_map/ppermute | solution.py:49
  101.3 15.0 %collective-permute-done.4 = bf16[768,384]{0,1:T(8,128)(2,1)} collective-permute-done((bf16[768,384]{0,1:T(8,128)(2,1)}, bf16[768,384]{0,1:T(8,128)(2,1)}, u32[]{:S(2)}, u32[]{:S(2)}) %collective-permute-start.4) | collective-permute-done | bytes 589856 | tf_op jit(solution)/shard_map/ppermute | solution.py:49
  116.3 1.9 constant_dynamic-update-slice_fusion.7
  118.2 1.9 constant_dynamic-update-slice_fusion.6
  121.9 1.9 constant_dynamic-update-slice_fusion.3
  123.8 1.9 constant_dynamic-update-slice_fusion.2
  127.4 7.4 %multiply_convert_fusion = (bf16[1024,768]{1,0:T(8,128)(2,1)}, f32[1024,768]{1,0:T(8,128)}) fusion(bf16[1024,1536]{1,0:T(8,128)(2,1)} %all-gather.4.cloned.1.call-done, bf16[1536,768]{1,0:T(8,128)(2,1)} %all-gather.6.cloned.1.call-done), kind=kOutput, calls=%fused_computation.92 | convolution fusion | flops 2419851264 | bytes 10223616 | tf_op jit(solution)/shard_map/dot_general | solution.py:75
  134.8 6.5 %convolution_convert_fusion = bf16[1024,1536]{1,0:T(8,128)(2,1)} fusion(bf16[1024,768]{1,0:T(8,128)(2,1)} %get-tuple-element.120, bf16[768,3072]{0,1:T(8,128)(2,1)} %constant_dynamic-update-slice_fusion, s32[]{:T(128)S(6)} %select_n.14), kind=kOutput, calls=%fused_computation.85 | convolution fusion | flops 2417491968 | bytes 7077892 | tf_op jit(solution)/shard_map/dot_general | solution.py:77
  141.4 46.5 %reduce-scatter.5.cloned.1.call-done = bf16[128,1536]{1,0:T(8,128)(2,1)} async-done(((bf16[1024,1536]{1,0:T(8,128)(2,1)}), bf16[128,1536]{1,0:T(8,128)(2,1)}) %reduce-scatter.5.cloned.1.call-update) | async-done | bytes 393232 | tf_op jit(solution)/shard_map/reduce_scatter | solution.py:78
  187.9 2.7 fusion.13
  190.9 32.6 %all-gather.8.cloned.1.call-done = bf16[1024,1536]{1,0:T(8,128)(2,1)} async-done(((bf16[128,1536]{1,0:T(8,128)(2,1)}), bf16[1024,1536]{1,0:T(8,128)(2,1)}) %all-gather.8.cloned.1.call-update) | async-done | bytes 3145744 | tf_op jit(solution)/shard_map/all_gather | solution.py:56
  223.5 7.2 %fusion.115 = f32[768,1536]{1,0:T(8,128)} fusion(bf16[1024,768]{1,0:T(8,128)(2,1)} %get-tuple-element.120, bf16[1024,1536]{1,0:T(8,128)(2,1)} %all-gather.8.cloned.1.call-done), kind=kOutput, calls=%fused_computation.333 | convolution fusion | flops 2415919104 | bytes 9437184 | tf_op jit(solution)/shard_map/dot_general | solution.py:84
  230.8 6.9 %fusion.5 = bf16[1024,768]{1,0:T(8,128)(2,1)S(1)} fusion(f32[1024,768]{1,0:T(8,128)} %get-tuple-element.121, bf16[1024,1536]{1,0:T(8,128)(2,1)} %all-gather.8.cloned.1.call-done, bf16[768,3072]{0,1:T(8,128)(2,1)} %constant_dynamic-update-slice_fusion, s32[]{:T(128)S(6)} %select_n.14), kind=kOutput, calls=%fused_computation.91 | convolution fusion | flops 2423783424 | bytes 10223620 | tf_op jit(solution)/shard_map/dot_general | solution.py:85
  237.7 1.2 copy-done.53
  238.9 4.6 fusion.113
  243.5 7.2 %fusion.114 = f32[1536,768]{1,0:T(8,128)} fusion(bf16[1024,1536]{1,0:T(8,128)(2,1)} %all-gather.4.cloned.1.call-done, bf16[1024,768]{1,0:T(8,128)(2,1)} %copy-done.53), kind=kOutput, calls=%fused_computation.332 | convolution fusion | flops 2415919104 | bytes 9437184 | tf_op jit(solution)/shard_map/dot_general | solution.py:89
  250.8 64.9 %reduce-scatter.11.cloned.1.call-done = f32[768,384]{1,0:T(8,128)} async-done(((f32[768,1536]{1,0:T(8,128)}), f32[768,384]{1,0:T(8,128)}) %reduce-scatter.11.cloned.1.call-update) | async-done | bytes 1179664 | tf_op jit(solution)/shard_map/reduce_scatter | solution.py:98
  315.8 2.7 copy.26
  318.4 4.9 all-to-all-start.3
  323.3 58.3 %reduce-scatter.7.cloned.1.call-done = f32[128,1536]{1,0:T(8,128)} async-done(((f32[1024,1536]{1,0:T(8,128)}), f32[128,1536]{1,0:T(8,128)}) %reduce-scatter.7.cloned.1.call-update) | async-done | bytes 786448 | tf_op jit(solution)/shard_map/reduce_scatter | solution.py:95
  381.6 2.0 multiply_reduce_fusion
  383.7 3.6 multiply_reduce_fusion.2
  387.3 2.0 multiply_reduce_fusion.1
  401.6 3.6 collective-permute-start.5
  405.2 1.9 collective-permute-start.6
  407.1 1.1 multiply_reduce_fusion.3
  408.7 4.2 stack.199
  413.7 46.1 %all-reduce.2 = (f32[1536]{0:T(1024)}, f32[1536]{0:T(1024)}) all-reduce(f32[1536]{0:T(1024)} %get-tuple-element.56, f32[1536]{0:T(1024)} %get-tuple-element.113), channel_id=1, replica_groups=mesh['dp'=4,'fsdp'=2,'rows'=4] {'dp','fsdp','rows'}, use_global_device_ids=true, to_apply=%region_59.60 | all-reduce | flops 3072 | bytes 24576 | tf_op jit(solution)/shard_map/psum | solution.py:125
  459.8 1.1 maximum_convert_fusion.1
  460.9 9.4 %reduce-scatter.9.cloned.1.call-done = f32[384,768]{1,0:T(8,128)} async-done(((f32[1536,768]{1,0:T(8,128)}), f32[384,768]{1,0:T(8,128)}) %reduce-scatter.9.cloned.1.call-update) | async-done | bytes 1179664 | tf_op jit(solution)/shard_map/reduce_scatter | solution.py:96
  470.3 4.1 all-to-all-start.2
  474.4 8.0 %fusion.101 = bf16[1,4,32,1536]{3,2,1,0:T(8,128)(2,1)} fusion(f32[1,10,32,1536]{3,2,1,0:T(8,128)S(1)} %maximum_convert_fusion.1, bf16[1,4,32,1536]{3,2,1,0:T(8,128)(2,1)S(1)} %copy-done.4, f32[1536]{0:T(1024)} %copy-done.17, f32[1536]{0:T(1024)} %copy-done.18, f32[1536]{0:T(1024)} %copy-done.20, f32[1536]{0:T(1024)} %copy-done.21, f32[1536]{0:T(1024)} %copy-done.22, ...), kind=kLoop, calls=%fused_computation.191 | loop fusion | flops 19660800 | bytes 8562688 | tf_op jit(solution)/shard_map/convert_element_type | solution.py:124
  482.4 2.4 copy.31
  484.8 5.2 all-to-all-done.2
  490.0 1.1 copy.30
  491.1 112.3 %all-reduce.5.cloned.1.call-done = f32[7,7,1536]{2,1,0:T(8,128)} async-done(((f32[7,7,1536]{2,1,0:T(8,128)}), f32[7,7,1536]{2,1,0:T(8,128)}) %all-reduce.5.cloned.1.call-update) | async-done | bytes 301072 | tf_op jit(solution)/shard_map/psum | solution.py:125
  603.5 1.7 copy.44
  (199 shorter events, 19.5 us)
Async XLA Ops:
  7.2 14.3 %copy-start = (bf16[1,4,32,1536]{3,2,1,0:T(8,128)(2,1)S(1)}, bf16[1,4,32,1536]{3,2,1,0:T(8,128)(2,1)}, u32[]{:S(2)}) copy-start(bf16[1,4,32,1536]{3,2,1,0:T(8,128)(2,1)} %param.7) | copy-start | bytes 1179652
  7.2 18.9 %copy-start.6 = (f32[7,7,1536]{2,1,0:T(8,128)S(1)}, f32[7,7,1536]{2,1,0:T(8,128)}, u32[]{:S(2)}) copy-start(f32[7,7,1536]{2,1,0:T(8,128)} %param.8) | copy-start | bytes 903172
  7.2 120.2 %all-gather.6.cloned.1.call-start = ((), (), s32[]{:S(2)}) async-start(), calls=%async_computation.9 | async-start | bytes 2949120 | tf_op jit(solution)/shard_map/all_gather | solution.py:42
  21.4 106.0 %all-gather.4.cloned.1.call-start = ((), (), s32[]{:S(2)}) async-start(), calls=%async_computation.8 | async-start | bytes 3538944 | tf_op jit(solution)/shard_map/all_gather | solution.py:74
  21.5 6.3 %collective-permute-start = (bf16[1,3,32,1536]{3,2,1,0:T(8,128)(2,1)S(1)}, bf16[1,3,32,1536]{3,2,1,0:T(8,128)(2,1)S(1)}, u32[]{:S(2)}, u32[]{:S(2)}) collective-permute-start(bf16[1,3,32,1536]{3,2,1,0:T(8,128)(2,1)S(1)} %get-tuple-element.118), channel_id=1, source_target_pairs={{0,1},{1,2},{2,3},{4,5},{5,6},{6,7},{8,9},{9,10},{10,11},{12,13},{... | collective-permute-start | bytes 884744 | tf_op jit(solution)/shard_map/ppermute | solution.py:22
  24.2 8.0 %collective-permute-start.1 = (bf16[1,3,32,1536]{3,2,1,0:T(8,128)(2,1)S(1)}, bf16[1,3,32,1536]{3,2,1,0:T(8,128)(2,1)S(1)}, u32[]{:S(2)}, u32[]{:S(2)}) collective-permute-start(bf16[1,3,32,1536]{3,2,1,0:T(8,128)(2,1)S(1)} %get-tuple-element.119), channel_id=1, source_target_pairs={{1,0},{2,1},{3,2},{5,4},{6,5},{7,6},{9,8},{10,9},{11,10},{13,12},{... | collective-permute-start | bytes 884744 | tf_op jit(solution)/shard_map/ppermute | solution.py:23
  26.3 6.1 copy-start.8
  26.3 6.1 copy-start.10
  26.3 6.1 copy-start.11
  26.3 6.1 copy-start.12
  26.3 6.1 copy-start.13
  26.3 6.1 copy-start.14
  26.4 6.1 copy-start.15
  26.4 6.1 copy-start.16
  26.4 6.1 copy-start.17
  26.4 6.1 copy-start.18
  26.7 5.7 copy-start.19
  26.7 5.7 copy-start.20
  26.7 5.7 copy-start.21
  26.7 5.7 copy-start.22
  26.8 5.7 copy-start.23
  26.8 5.7 copy-start.24
  26.8 5.7 copy-start.25
  26.8 5.7 copy-start.26
  26.8 5.7 copy-start.27
  32.7 9.9 %copy-start.7 = (f32[1536]{0:T(1024)S(1)}, f32[1536]{0:T(1024)}, u32[]{:S(2)}) copy-start(f32[1536]{0:T(1024)} %param.9) | copy-start | bytes 18436
  42.3 75.9 %copy-start.48 = (f32[128]{0:T(128)}, f32[128]{0:T(128)S(1)}, u32[]{:S(2)}) copy-start(f32[128]{0:T(128)S(1)} %div.15) | copy-start | bytes 1540
  42.6 75.6 %copy-start.50 = (f32[128]{0:T(128)}, f32[128]{0:T(128)S(1)}, u32[]{:S(2)}) copy-start(f32[128]{0:T(128)S(1)} %rsqrt.12) | copy-start | bytes 1540
  43.6 144.3 %reduce-scatter.5.cloned.1.call-start = ((), (), s32[]{:S(2)}) async-start(), calls=%async_computation.10 | async-start | bytes 3538944 | tf_op jit(solution)/shard_map/reduce_scatter | solution.py:78
  54.4 30.4 %collective-permute-start.2 = (bf16[768,384]{0,1:T(8,128)(2,1)S(1)}, bf16[768,384]{0,1:T(8,128)(2,1)S(1)}, u32[]{:S(2)}, u32[]{:S(2)}) collective-permute-start(bf16[768,384]{0,1:T(8,128)(2,1)S(1)} %bitcast.106), channel_id=1, source_target_pairs={{0,8},{8,16},{16,24},{24,0},{1,9},{9,17},{17,25},{25,1},{2,10},{10... | collective-permute-start | bytes 1769480 | tf_op jit(solution)/shard_map/ppermute | solution.py:49
  85.6 15.7 %collective-permute-start.3 = (bf16[768,384]{0,1:T(8,128)(2,1)S(1)}, bf16[768,384]{0,1:T(8,128)(2,1)}, u32[]{:S(2)}, u32[]{:S(2)}) collective-permute-start(bf16[768,384]{0,1:T(8,128)(2,1)S(1)} %collective-permute-done.2), channel_id=1, source_target_pairs={{0,8},{8,16},{16,24},{24,0},{1,9},{9,17},{17,25},{25,1},{2,10},{10... | collective-permute-start | bytes 1769480 | tf_op jit(solution)/shard_map/ppermute | solution.py:49
  101.3 15.0 %collective-permute-start.4 = (bf16[768,384]{0,1:T(8,128)(2,1)}, bf16[768,384]{0,1:T(8,128)(2,1)}, u32[]{:S(2)}, u32[]{:S(2)}) collective-permute-start(bf16[768,384]{0,1:T(8,128)(2,1)} %collective-permute-done.3), channel_id=1, source_target_pairs={{0,8},{8,16},{16,24},{24,0},{1,9},{9,17},{17,25},{25,1},{2,10},{10... | collective-permute-start | bytes 1769480 | tf_op jit(solution)/shard_map/ppermute | solution.py:49
  101.3 18.8 %copy-start.3 = (bf16[768,384]{0,1:T(8,128)(2,1)S(1)}, bf16[768,384]{0,1:T(8,128)(2,1)}, u32[]{:S(2)}) copy-start(bf16[768,384]{0,1:T(8,128)(2,1)} %copy-done.2) | copy-start | bytes 1769476
  141.3 46.6 %copy-start.1 = (bf16[1,4,32,1536]{3,2,1,0:T(8,128)(2,1)S(1)}, bf16[1,4,32,1536]{3,2,1,0:T(8,128)(2,1)}, u32[]{:S(2)}) copy-start(bf16[1,4,32,1536]{3,2,1,0:T(8,128)(2,1)} %param.7) | copy-start | bytes 1179652
  141.3 46.6 %copy-start.4 = (bf16[1,4,32,1536]{3,2,1,0:T(8,128)(2,1)S(1)}, bf16[1,4,32,1536]{3,2,1,0:T(8,128)(2,1)}, u32[]{:S(2)}) copy-start(bf16[1,4,32,1536]{3,2,1,0:T(8,128)(2,1)} %param.13) | copy-start | bytes 1179652
  141.4 82.1 %all-gather.8.cloned.1.call-start = ((), (), s32[]{:S(2)}) async-start(), calls=%async_computation.11 | async-start | bytes 3538944 | tf_op jit(solution)/shard_map/all_gather | solution.py:56
  190.6 125.2 %reduce-scatter.11.cloned.1.call-start = ((), (), s32[]{:S(2)}) async-start(), calls=%async_computation.14 | async-start | bytes 5898240 | tf_op jit(solution)/shard_map/reduce_scatter | solution.py:98
  230.7 150.9 %reduce-scatter.7.cloned.1.call-start = ((), (), s32[]{:S(2)}) async-start(), calls=%async_computation.12 | async-start | bytes 7077888 | tf_op jit(solution)/shard_map/reduce_scatter | solution.py:95
  230.8 8.1 %copy-start.52 = (bf16[1536,768]{1,0:T(8,128)(2,1)S(1)}, bf16[1536,768]{1,0:T(8,128)(2,1)}, u32[]{:S(2)}) copy-start(bf16[1536,768]{1,0:T(8,128)(2,1)} %all-gather.6.cloned.1.call-done) | copy-start | bytes 7077892
  243.5 226.8 %reduce-scatter.9.cloned.1.call-start = ((), (), s32[]{:S(2)}) async-start(), calls=%async_computation.13 | async-start | bytes 5898240 | tf_op jit(solution)/shard_map/reduce_scatter | solution.py:96
  250.8 130.8 %copy-start.49 = (f32[128]{0:T(128)S(1)}, f32[128]{0:T(128)}, u32[]{:S(2)}) copy-start(f32[128]{0:T(128)} %copy-done.48) | copy-start | bytes 1540
  250.8 130.8 %copy-start.51 = (f32[128]{0:T(128)S(1)}, f32[128]{0:T(128)}, u32[]{:S(2)}) copy-start(f32[128]{0:T(128)} %copy-done.50) | copy-start | bytes 1540
  318.4 151.9 %all-to-all-start.3 = ((f32[768,4,96]{0,2,1:T(8,128)}), f32[768,4,96]{0,2,1:T(8,128)}, u32[]{:S(2)}, u32[]{:S(2)}) async-start(f32[768,4,96]{0,2,1:T(8,128)} %bitcast.109), calls=%async_computation.7 | async-start | bytes 2359296 | tf_op jit(solution)/shard_map/all_to_all | solution.py:99
  323.3 280.2 %all-reduce.5.cloned.1.call-start = ((), (), s32[]{:S(2)}) async-start(), calls=%async_computation.15 | async-start | bytes 688128 | tf_op jit(solution)/shard_map/psum | solution.py:125
  401.6 58.2 %collective-permute-start.5 = (bf16[1,3,32,1536]{3,2,1,0:T(8,128)(2,1)}, bf16[1,3,32,1536]{3,2,1,0:T(8,128)(2,1)S(1)}, u32[]{:S(2)}, u32[]{:S(2)}) collective-permute-start(bf16[1,3,32,1536]{3,2,1,0:T(8,128)(2,1)} %get-tuple-element.116), channel_id=1, source_target_pairs={{0,1},{1,2},{2,3},{4,5},{5,6},{6,7},{8,9},{9,10},{10,11},{12,13},{... | collective-permute-start | bytes 884744 | tf_op jit(solution)/shard_map/ppermute | solution.py:22
  405.2 54.6 %collective-permute-start.6 = (bf16[1,3,32,1536]{3,2,1,0:T(8,128)(2,1)}, bf16[1,3,32,1536]{3,2,1,0:T(8,128)(2,1)}, u32[]{:S(2)}, u32[]{:S(2)}) collective-permute-start(bf16[1,3,32,1536]{3,2,1,0:T(8,128)(2,1)} %get-tuple-element.117), channel_id=1, source_target_pairs={{1,0},{2,1},{3,2},{5,4},{6,5},{7,6},{9,8},{10,9},{11,10},{13,12},{... | collective-permute-start | bytes 884744 | tf_op jit(solution)/shard_map/ppermute | solution.py:23
  459.8 14.6 %copy-start.9 = (f32[1536]{0:T(1024)S(1)}, f32[1536]{0:T(1024)}, u32[]{:S(2)}) copy-start(f32[1536]{0:T(1024)} %copy-done.8) | copy-start | bytes 18436
  470.3 19.7 %all-to-all-start.2 = ((f32[4,96,768]{2,1,0:T(8,128)}), f32[4,96,768]{2,1,0:T(8,128)S(1)}, u32[]{:S(2)}, u32[]{:S(2)}) async-start(f32[4,96,768]{2,1,0:T(8,128)} %bitcast.115), calls=%async_computation.5 | async-start | bytes 2359296 | tf_op jit(solution)/shard_map/all_to_all | solution.py:97
  (23 other events, 109.5 us)
Sparse Core Ops, SparseCore 0:
  21.5 63.6 all-gather.5
  87.7 31.6 all-gather.3
  141.5 46.3 reduce-scatter.4
  190.7 32.6 all-gather.7
  230.8 84.8 reduce-scatter.10
  319.4 62.1 reduce-scatter.6
  383.9 86.3 reduce-scatter.8
  476.2 127.2 all-reduce.4
